TPU v7x, 512 devices: a whole 4x8x8 slice. The times are simulated.
512 devices in a mesh: member: 16 (over x_lo, y), dp: 32 (over z, x_hi, core).
Axes of the slice: x: 4 (x_hi: 2, x_lo: 2; x = x_hi * 2 + x_lo), y: 8, z: 8, core: 2. Of those that a mesh axis runs over, the one named last changes fastest.
Arguments:
- inputs: bfloat16 [8192, 64], P('dp'), may hold values from -6 to 6
- observed: float32 [64, 8192], P('member', 'dp'), may hold values from -6 to 6
- noise: bfloat16 [2, 32, 64, 8192], P(None, None, 'member', 'dp'), may hold values from -4 to 4
- w_in: float32 [32, 64, 4096], P('member', None, 'dp'), may hold values from -0.75 to 0.75
- b_in: float32 [32, 4096], P('member', 'dp'), may hold values from -3 to 3
- w_out: float32 [32, 64, 4096], P('member', None, 'dp'), may hold values from -0.09375 to 0.09375
- b_out: float32 [32, 64], P('member'), may hold values from -3 to 3
Outputs:
- new_w_in: float32 [32, 64, 4096], P('member', None, 'dp')
- new_b_in: float32 [32, 4096], P('member', 'dp')
- new_w_out: float32 [32, 64, 4096], P('member', None, 'dp')
- new_b_out: float32 [32, 64], P('member')
All inputs are finite; a program needn't handle non-finite values.
Results may differ from a plain program's by a relative error of at most 0.00056.
Values may be sent and summed in bfloat16 or wider, within the bound.
No kernel may reach another device: no remote copies, remote signals or barrier semaphores. Data moves between devices by JAX's collectives and lax.ppermute only.
A program may use at most 64 MiB of HBM per device.

v0:
```python
import jax
import jax.numpy as jnp
from jax import lax
from jax.sharding import PartitionSpec as P

UPDATES = 2
ridge_level = 0.5


def solve_gain(gram, cross):
    eye = jnp.eye(gram.shape[0], dtype=gram.dtype)
    factor = jnp.linalg.cholesky(gram + ridge_level * eye)
    middle = lax.linalg.triangular_solve(factor, cross, left_side=True, lower=True)
    return lax.linalg.triangular_solve(factor, middle, left_side=True, lower=True, transpose_a=True)


def pack(w_in, b_in, w_out, b_out):
    n = w_in.shape[0]
    return jnp.concatenate(
        [w_in.reshape(n, -1), w_out.reshape(n, -1), b_in.reshape(n, -1), b_out.reshape(n, -1)],
        axis=1,
    )


def unpack(flat, f_in, hid, outs):
    n = flat.shape[0]
    a = f_in * hid
    b = a + outs * hid
    c = b + hid
    return (
        flat[:, :a].reshape(n, f_in, hid),
        flat[:, b:c].reshape(n, hid),
        flat[:, a:b].reshape(n, outs, hid),
        flat[:, c:].reshape(n, outs),
    )


def predict(inputs, own_flat, b_out, f_in, hid, outs):
    n = own_flat.shape[0]
    a = f_in * hid
    b = a + outs * hid
    rounded = own_flat[:, : b + hid].astype(jnp.bfloat16)
    gathered = lax.all_gather(rounded, "dp", axis=0, tiled=False)
    d = gathered.shape[0]
    w_in = gathered[:, :, :a].reshape(d, n, f_in, hid)
    w_out = gathered[:, :, a:b].reshape(d, n, outs, hid)
    b_in = gathered[:, :, b : b + hid]
    pre = jnp.einsum("sf,dnfh->nsdh", inputs, w_in, preferred_element_type=jnp.float32)
    pre = pre + jnp.transpose(b_in, (1, 0, 2)).astype(jnp.float32)[:, None, :, :]
    hidden = jnp.tanh(pre).astype(jnp.bfloat16)
    pred = jnp.einsum("dnoh,nsdh->nos", w_out, hidden, preferred_element_type=jnp.float32)
    return pred + b_out[:, :, None]


def on_device(inputs, observed, noise, w_in, b_in, w_out, b_out):
    per_device = w_in.shape[0]
    f_in, hid = (w_in.shape[1], w_in.shape[2])
    outs = w_out.shape[1]
    count = observed.shape[0] * lax.axis_size("member") * observed.shape[1] * lax.axis_size("dp")
    first = lax.axis_index("member") * per_device
    own = pack(w_in, b_in, w_out, b_out)
    whole = lax.all_gather(own, "member", axis=0, tiled=True)
    for update in range(UPDATES):
        own_b_out = own[:, -outs:]
        predicted = predict(inputs, own, own_b_out, f_in, hid, outs)
        collected = lax.all_to_all(predicted, "member", split_axis=1, concat_axis=0, tiled=True)
        mean_pred = jnp.mean(collected, axis=0)
        anomaly = (collected - mean_pred[None]).reshape(collected.shape[0], -1)
        misfit = (observed[None] + noise[update].astype(jnp.float32) - collected).reshape(
            collected.shape[0], -1
        )
        gram_part = lax.dot_general(
            anomaly, anomaly, (((1,), (1,)), ((), ())), precision=lax.Precision.HIGHEST
        )
        cross_part = lax.dot_general(
            anomaly, misfit, (((1,), (1,)), ((), ())), precision=lax.Precision.HIGHEST
        )
        gram, cross = lax.psum((gram_part, cross_part), ("member", "dp"))
        gain = solve_gain(gram / count, cross / count)
        if update + 1 < UPDATES:
            moved = lax.dot_general(
                gain, whole, (((0,), (0,)), ((), ())), precision=lax.Precision.HIGHEST
            )
            whole = whole + moved
            own = lax.dynamic_slice_in_dim(whole, first, per_device, 0)
        else:
            columns = lax.dynamic_slice_in_dim(gain, first, per_device, 1)
            moved = lax.dot_general(
                columns, whole, (((0,), (0,)), ((), ())), precision=lax.Precision.HIGHEST
            )
            own = own + moved
    return unpack(own, f_in, hid, outs)


def solution(mesh):
    placed = (
        P("dp", None),
        P("member", "dp"),
        P(None, None, "member", "dp"),
        P("member", None, "dp"),
        P("member", "dp"),
        P("member", None, "dp"),
        P("member", None),
    )
    return jax.shard_map(
        on_device,
        mesh=mesh,
        in_specs=placed,
        out_specs=(
            P("member", None, "dp"),
            P("member", "dp"),
            P("member", None, "dp"),
            P("member", None),
        ),
        check_vma=False,
    )
```

profile of v0, /device:TPU:1, one launch (start us, length us, event | category | flops | bytes accessed | tf_op | source)
XLA Modules:
  0.0 511.3 jit_solution(14198276268625181387)
XLA Ops:
  7.2 0.0 copy-start
  7.2 0.0 all-gather.7.cloned.1.call-start
  7.2 0.7 convert_bitcast_fusion.2
  7.9 0.8 convert.20
  8.8 0.8 convert.19
  9.6 0.7 pad_maximum_fusion
  10.3 0.0 all-gather.7.cloned.1.call-update
  10.3 0.0 all-gather.9.cloned.1.call-start
  10.4 1.0 copy_bitcast_fusion.2
  11.4 1.4 maximum_bitcast_fusion
  12.8 0.0 all-gather.9.cloned.1.call-update
  12.8 90.6 %all-gather.7.cloned.1.call-done = bf16[32,2,16512]{2,1,0:T(2,128)(2,1)} async-done(((bf16[1,2,16512]{2,1,0:T(2,128)(2,1)}), bf16[32,2,16512]{2,1,0:T(2,128)(2,1)}) %all-gather.7.cloned.1.call-update) | async-done | bytes 2113552 | tf_op jit(solution)/shard_map/all_gather | solution.py:43
  103.4 0.7 convert_bitcast_fusion.1
  104.1 2.9 fusion.60
  107.1 0.8 reshape.148
  107.9 0.8 reshape.147
  108.8 2.5 fusion.20
  111.3 0.7 copy.43
  112.1 6.6 %all-to-all-start = ((f32[2,64,256]{2,0,1:T(2,128)}), f32[2,64,256]{2,0,1:T(2,128)S(1)}, u32[]{:S(2)}, u32[]{:S(2)}) async-start(f32[2,64,256]{2,0,1:T(2,128)} %copy.43), calls=%async_computation | async-start | bytes 262144 | tf_op jit(solution)/shard_map/all_to_all | solution.py:66
  118.6 0.0 all-gather.11.cloned.1.call-start
  118.8 47.6 %all-gather.9.cloned.1.call-done = f32[16,2,16576]{2,1,0:T(2,128)} async-done(((f32[1,2,16576]{2,1,0:T(2,128)}), f32[16,2,16576]{2,1,0:T(2,128)}) %all-gather.9.cloned.1.call-update) | async-done | bytes 2121744 | tf_op jit(solution)/shard_map/all_gather | solution.py:62
  166.4 3.7 reshape.128
  170.0 0.1 bitcast_reduce_fusion.1
  170.1 0.1 fusion.28
  170.2 0.3 convolution_bitcast_fusion.3
  170.4 0.3 convolution_bitcast_fusion.2
  170.7 107.1 %all-reduce.1 = (f32[32,32]{0,1:T(8,128)S(1)}, f32[32,32]{0,1:T(8,128)S(1)}) all-reduce(f32[32,32]{0,1:T(8,128)S(1)} %convolution_bitcast_fusion.3, f32[32,32]{0,1:T(8,128)S(1)} %convolution_bitcast_fusion.2), channel_id=1, replica_groups=mesh['member'=16,'dp'=32] {'member','dp'}, use_global_device_ids=true, to_apply=%region_1.0 | all-reduce | flops 2048 | bytes 16384 | tf_op jit(solution)/shard_map/psum | solution.py:78
  277.8 0.1 copy.48
  277.9 2.9 cholesky.44
  280.8 0.6 compare_reduce_fusion.1
  281.5 0.7 fusion.39
  282.1 2.4 custom-call.11
  284.6 0.2 fusion.46
  284.8 0.1 fusion.48
  285.0 4.2 convolution_add_fusion
  289.1 0.7 fusion.35
  289.8 0.0 all-gather.11.cloned.1.call-update
  289.8 0.1 dynamic-slice.1
  289.9 80.4 %all-gather.11.cloned.1.call-done = bf16[32,2,16512]{2,1,0:T(2,128)(2,1)} async-done(((bf16[1,2,16512]{2,1,0:T(2,128)(2,1)}), bf16[32,2,16512]{2,1,0:T(2,128)(2,1)}) %all-gather.11.cloned.1.call-update) | async-done | bytes 2113552 | tf_op jit(solution)/shard_map/all_gather | solution.py:43
  370.3 4.0 fusion.59
  374.4 2.6 reshape.116
  377.0 0.7 convert_bitcast_fusion
  377.8 1.6 reshape.149
  379.4 3.2 fusion.1
  382.6 0.8 fusion.17
  383.5 0.1 copy.55
  383.6 13.8 %all_to_all.30 = f32[2,64,256]{2,0,1:T(2,128)S(1)} all-to-all(f32[2,64,256]{2,0,1:T(2,128)S(1)} %copy.55), channel_id=1, replica_groups=mesh['member'=16,'dp'=32] {'member'}, dimensions={1} | all-to-all | bytes 262144 | tf_op jit(solution)/shard_map/all_to_all | solution.py:66
  397.4 0.1 bitcast_reduce_fusion
  397.4 0.1 fusion.27
  397.5 0.2 convolution_bitcast_fusion.1
  397.8 0.3 convolution_bitcast_fusion
  398.0 96.0 %all-reduce = (f32[32,32]{0,1:T(8,128)S(1)}, f32[32,32]{0,1:T(8,128)S(1)}) all-reduce(f32[32,32]{0,1:T(8,128)S(1)} %convolution_bitcast_fusion.1, f32[32,32]{0,1:T(8,128)S(1)} %convolution_bitcast_fusion), channel_id=1, replica_groups=mesh['member'=16,'dp'=32] {'member','dp'}, use_global_device_ids=true, to_apply=%region_6.10 | all-reduce | flops 2048 | bytes 16384 | tf_op jit(solution)/shard_map/psum | solution.py:78
  494.0 0.1 copy.60
  494.1 2.9 cholesky.55
  497.1 0.6 compare_reduce_fusion
  497.7 0.7 fusion.40
  498.4 2.4 custom-call.13
  500.8 0.2 fusion.41
  501.0 0.2 fusion.43
  501.3 1.1 convolution_add_fusion.1
  502.4 0.6 slice.74
  503.0 0.6 slice.76
  503.5 0.6 copy.119
  504.2 0.6 copy.118
  (24 shorter events, 0.2 us)
Async XLA Ops:
  7.2 101.6 %copy-start = (bf16[256,64]{0,1:T(8,128)(2,1)S(1)}, bf16[256,64]{0,1:T(8,128)(2,1)}, u32[]{:S(2)}) copy-start(bf16[256,64]{0,1:T(8,128)(2,1)} %param.12) | copy-start | bytes 98308
  7.2 96.2 %all-gather.7.cloned.1.call-start = ((), (), s32[]{:S(2)}) async-start(), calls=%async_computation.2 | async-start | bytes 2179584 | tf_op jit(solution)/shard_map/all_gather | solution.py:43
  10.3 156.0 %all-gather.9.cloned.1.call-start = ((), (), s32[]{:S(2)}) async-start(), calls=%async_computation.3 | async-start | bytes 2263040 | tf_op jit(solution)/shard_map/all_gather | solution.py:62
  107.1 1.7 copy-start.4
  108.8 9.9 %copy-start.2 = (bf16[2,32,4,256]{3,2,1,0:T(4,128)(2,1)S(1)}, bf16[2,32,4,256]{3,2,1,0:T(4,128)(2,1)}, u32[]{:S(2)}) copy-start(bf16[2,32,4,256]{3,2,1,0:T(4,128)(2,1)} %param.14) | copy-start | bytes 393220
  112.1 58.0 %all-to-all-start = ((f32[2,64,256]{2,0,1:T(2,128)}), f32[2,64,256]{2,0,1:T(2,128)S(1)}, u32[]{:S(2)}, u32[]{:S(2)}) async-start(f32[2,64,256]{2,0,1:T(2,128)} %copy.43), calls=%async_computation | async-start | bytes 262144 | tf_op jit(solution)/shard_map/all_to_all | solution.py:66
  118.6 251.7 %all-gather.11.cloned.1.call-start = ((), (), s32[]{:S(2)}) async-start(), calls=%async_computation.4 | async-start | bytes 2179584 | tf_op jit(solution)/shard_map/all_gather | solution.py:43
  118.7 51.4 %copy-start.3 = (f32[4,256]{1,0:T(4,128)S(1)}, f32[4,256]{1,0:T(4,128)}, u32[]{:S(2)}) copy-start(f32[4,256]{1,0:T(4,128)} %param.13) | copy-start | bytes 12292
  379.4 3.2 copy-start.1
Sparse Core Ops, SparseCore 0:
  11.4 91.9 all-gather.6
  105.5 60.8 all-gather.8
  290.0 80.3 all-gather.10
where the time goes:
time: 512 us; the launch traced here: 511 us
  waiting for transfers between devices  219 us (43%)
  blocking collectives  217 us (42%)
  local copies, waits for them, and re-layouts  21.8 us (4%)
  other arithmetic  19.5 us (4%)
  between operations  14 us (3%)
  matrix products  13.7 us (3%)
  starting transfers between devices  6.69 us (1%)
    psum x2, blocking collectives, on_device(): gram, cross = lax.psum((gram_part, cross_part), ('member', 'dp'))  203 us
    all_gather x2, waiting for transfers between devices, predict(): gathered = lax.all_gather(rounded, 'dp', axis=0, tiled=False)  171 us
    all_gather x1, waiting for transfers between devices, on_device(): whole = lax.all_gather(own, 'member', axis=0, tiled=True)  47.6 us
    all_to_all x1, blocking collectives, on_device(): lax.all_to_all(predicted, 'member', split_axis=1, concat_axis=0, tiled=True)  13.8 us
  transfers between devices with their start and end apart: 4, of which 3 were waited for; matrix products, arithmetic and copies ran while one was open for 3% of the time, Pallas kernels for 0%

commit v1 on v0

--- a/solution.py
+++ b/solution.py
@@ -75,7 +75,7 @@
         cross_part = lax.dot_general(
             anomaly, misfit, (((1,), (1,)), ((), ())), precision=lax.Precision.HIGHEST
         )
-        gram, cross = lax.psum((gram_part, cross_part), ("member", "dp"))
+        gram, cross = lax.psum(lax.psum((gram_part, cross_part), "dp"), "member")
         gain = solve_gain(gram / count, cross / count)
         if update + 1 < UPDATES:
             moved = lax.dot_general(

time: 512 us -> 701 us (1.37)
  the two profiles are of different devices: /device:TPU:1 before, /device:TPU:2 now
where the time goes in v1:
time: 701 us
  blocking collectives  398 us (57%)
  waiting for transfers between devices  225 us (32%)
  local copies, waits for them, and re-layouts  21.9 us (3%)
  other arithmetic  19.6 us (3%)
  between operations  14 us (2%)
  matrix products  13.7 us (2%)
  starting transfers between devices  8.33 us (1%)
    psum x4, blocking collectives, on_device(): gram, cross = lax.psum(lax.psum((gram_part, cross_part), 'dp'), 'member')  382 us
    all_gather x2, waiting for transfers between devices, predict(): gathered = lax.all_gather(rounded, 'dp', axis=0, tiled=False)  168 us
    all_gather x1, waiting for transfers between devices, on_device(): whole = lax.all_gather(own, 'member', axis=0, tiled=True)  57 us
    all_to_all x1, blocking collectives, on_device(): lax.all_to_all(predicted, 'member', split_axis=1, concat_axis=0, tiled=True)  15.9 us
  transfers between devices with their start and end apart: 4, of which 3 were waited for; matrix products, arithmetic and copies ran while one was open for 2% of the time, Pallas kernels for 0%

profile of v1, /device:TPU:2, one launch (start us, length us, event | category | flops | bytes accessed | tf_op | source)
XLA Modules:
  0.0 700.7 jit_solution(353811854179499886)
XLA Ops:
  7.2 0.0 all-gather.7.cloned.1.call-start
  7.2 0.7 convert_bitcast_fusion.2
  7.9 0.8 convert.20
  8.8 0.8 convert.19
  9.6 0.7 pad_maximum_fusion
  10.3 0.0 all-gather.9.cloned.1.call-start
  10.4 1.0 copy_bitcast_fusion.2
  11.4 1.4 maximum_bitcast_fusion
  12.8 0.0 all-gather.9.cloned.1.call-update
  12.8 88.4 %all-gather.7.cloned.1.call-done = bf16[32,2,16512]{2,1,0:T(2,128)(2,1)} async-done(((bf16[1,2,16512]{2,1,0:T(2,128)(2,1)}), bf16[32,2,16512]{2,1,0:T(2,128)(2,1)}) %all-gather.7.cloned.1.call-update) | async-done | bytes 2113552 | tf_op jit(solution)/shard_map/all_gather | solution.py:43
  101.2 0.7 convert_bitcast_fusion.1
  102.0 2.9 fusion.60
  104.9 0.8 reshape.148
  105.7 0.8 reshape.147
  106.6 2.5 fusion.20
  109.1 0.8 copy.43
  109.9 8.2 %all-to-all-start = ((f32[2,64,256]{2,0,1:T(2,128)}), f32[2,64,256]{2,0,1:T(2,128)S(1)}, u32[]{:S(2)}, u32[]{:S(2)}) async-start(f32[2,64,256]{2,0,1:T(2,128)} %copy.43), calls=%async_computation | async-start | bytes 262144 | tf_op jit(solution)/shard_map/all_to_all | solution.py:66
  118.1 0.0 all-gather.11.cloned.1.call-start
  118.2 57.0 %all-gather.9.cloned.1.call-done = f32[16,2,16576]{2,1,0:T(2,128)} async-done(((f32[1,2,16576]{2,1,0:T(2,128)}), f32[16,2,16576]{2,1,0:T(2,128)}) %all-gather.9.cloned.1.call-update) | async-done | bytes 2121744 | tf_op jit(solution)/shard_map/all_gather | solution.py:62
  175.3 3.7 reshape.128
  179.0 0.1 bitcast_reduce_fusion.1
  179.1 0.1 fusion.28
  179.1 0.2 convolution_bitcast_fusion.3
  179.4 0.3 convolution_bitcast_fusion.2
  179.6 128.5 %all-reduce.1 = (f32[32,32]{0,1:T(8,128)S(1)}, f32[32,32]{0,1:T(8,128)S(1)}) all-reduce(f32[32,32]{0,1:T(8,128)S(1)} %convolution_bitcast_fusion.3, f32[32,32]{0,1:T(8,128)S(1)} %convolution_bitcast_fusion.2), channel_id=1, replica_groups=mesh['member'=16,'dp'=32] {'dp'}, use_global_device_ids=true, to_apply=%region_1.0 | all-reduce | flops 2048 | bytes 16384 | tf_op jit(solution)/shard_map/psum | solution.py:78
  308.1 61.9 %all-reduce.3 = (f32[32,32]{0,1:T(8,128)S(1)}, f32[32,32]{0,1:T(8,128)S(1)}) all-reduce(f32[32,32]{0,1:T(8,128)S(1)} %get-tuple-element.9, f32[32,32]{0,1:T(8,128)S(1)} %get-tuple-element.10), channel_id=1, replica_groups=mesh['member'=16,'dp'=32] {'member'}, use_global_device_ids=true, to_apply=%region_2.0 | all-reduce | flops 2048 | bytes 16384 | tf_op jit(solution)/shard_map/psum | solution.py:78
  370.0 0.1 copy.48
  370.1 2.9 cholesky.44
  373.0 0.6 compare_reduce_fusion.1
  373.7 0.7 fusion.39
  374.3 2.4 custom-call.11
  376.8 0.2 fusion.46
  377.0 0.1 fusion.48
  377.1 4.2 convolution_add_fusion
  381.3 0.7 fusion.35
  382.0 0.0 all-gather.11.cloned.1.call-update
  382.0 0.1 dynamic-slice.1
  382.1 79.7 %all-gather.11.cloned.1.call-done = bf16[32,2,16512]{2,1,0:T(2,128)(2,1)} async-done(((bf16[1,2,16512]{2,1,0:T(2,128)(2,1)}), bf16[32,2,16512]{2,1,0:T(2,128)(2,1)}) %all-gather.11.cloned.1.call-update) | async-done | bytes 2113552 | tf_op jit(solution)/shard_map/all_gather | solution.py:43
  461.8 4.1 fusion.59
  465.8 2.6 reshape.116
  468.5 0.7 convert_bitcast_fusion
  469.2 1.6 reshape.149
  470.9 3.2 fusion.1
  474.1 0.8 fusion.17
  474.9 0.1 copy.55
  475.1 15.9 %all_to_all.30 = f32[2,64,256]{2,0,1:T(2,128)S(1)} all-to-all(f32[2,64,256]{2,0,1:T(2,128)S(1)} %copy.55), channel_id=1, replica_groups=mesh['member'=16,'dp'=32] {'member'}, dimensions={1} | all-to-all | bytes 262144 | tf_op jit(solution)/shard_map/all_to_all | solution.py:66
  491.0 0.1 bitcast_reduce_fusion
  491.0 0.1 fusion.27
  491.1 0.3 convolution_bitcast_fusion.1
  491.4 0.3 convolution_bitcast_fusion
  491.6 129.1 %all-reduce = (f32[32,32]{0,1:T(8,128)S(1)}, f32[32,32]{0,1:T(8,128)S(1)}) all-reduce(f32[32,32]{0,1:T(8,128)S(1)} %convolution_bitcast_fusion.1, f32[32,32]{0,1:T(8,128)S(1)} %convolution_bitcast_fusion), channel_id=1, replica_groups=mesh['member'=16,'dp'=32] {'dp'}, use_global_device_ids=true, to_apply=%region_8.12 | all-reduce | flops 2048 | bytes 16384 | tf_op jit(solution)/shard_map/psum | solution.py:78
  620.7 62.7 %all-reduce.2 = (f32[32,32]{0,1:T(8,128)S(1)}, f32[32,32]{0,1:T(8,128)S(1)}) all-reduce(f32[32,32]{0,1:T(8,128)S(1)} %get-tuple-element.7, f32[32,32]{0,1:T(8,128)S(1)} %get-tuple-element.8), channel_id=1, replica_groups=mesh['member'=16,'dp'=32] {'member'}, use_global_device_ids=true, to_apply=%region_9.13 | all-reduce | flops 2048 | bytes 16384 | tf_op jit(solution)/shard_map/psum | solution.py:78
  683.4 0.1 copy.60
  683.5 2.9 cholesky.55
  686.4 0.6 compare_reduce_fusion
  687.1 0.7 fusion.40
  687.7 2.4 custom-call.13
  690.1 0.2 fusion.41
  690.4 0.2 fusion.43
  690.6 1.1 convolution_add_fusion.1
  691.7 0.6 slice.74
  692.3 0.6 slice.76
  692.9 0.6 copy.119
  693.5 0.6 copy.118
  (26 shorter events, 0.3 us)
Async XLA Ops:
  7.2 99.4 %copy-start = (bf16[256,64]{0,1:T(8,128)(2,1)S(1)}, bf16[256,64]{0,1:T(8,128)(2,1)}, u32[]{:S(2)}) copy-start(bf16[256,64]{0,1:T(8,128)(2,1)} %param.12) | copy-start | bytes 98308
  7.2 94.0 %all-gather.7.cloned.1.call-start = ((), (), s32[]{:S(2)}) async-start(), calls=%async_computation.2 | async-start | bytes 2179584 | tf_op jit(solution)/shard_map/all_gather | solution.py:43
  10.3 164.9 %all-gather.9.cloned.1.call-start = ((), (), s32[]{:S(2)}) async-start(), calls=%async_computation.3 | async-start | bytes 2263040 | tf_op jit(solution)/shard_map/all_gather | solution.py:62
  104.9 1.7 copy-start.4
  106.6 11.6 %copy-start.2 = (bf16[2,32,4,256]{3,2,1,0:T(4,128)(2,1)S(1)}, bf16[2,32,4,256]{3,2,1,0:T(4,128)(2,1)}, u32[]{:S(2)}) copy-start(bf16[2,32,4,256]{3,2,1,0:T(4,128)(2,1)} %param.14) | copy-start | bytes 393220
  109.9 69.1 %all-to-all-start = ((f32[2,64,256]{2,0,1:T(2,128)}), f32[2,64,256]{2,0,1:T(2,128)S(1)}, u32[]{:S(2)}, u32[]{:S(2)}) async-start(f32[2,64,256]{2,0,1:T(2,128)} %copy.43), calls=%async_computation | async-start | bytes 262144 | tf_op jit(solution)/shard_map/all_to_all | solution.py:66
  118.1 343.7 %all-gather.11.cloned.1.call-start = ((), (), s32[]{:S(2)}) async-start(), calls=%async_computation.4 | async-start | bytes 2179584 | tf_op jit(solution)/shard_map/all_gather | solution.py:43
  118.2 60.8 %copy-start.3 = (f32[4,256]{1,0:T(4,128)S(1)}, f32[4,256]{1,0:T(4,128)}, u32[]{:S(2)}) copy-start(f32[4,256]{1,0:T(4,128)} %param.13) | copy-start | bytes 12292
  470.9 3.2 copy-start.1
Sparse Core Ops, SparseCore 0:
  11.4 89.7 all-gather.6
  103.3 71.9 all-gather.8
  382.2 79.5 all-gather.10
